TPU v7x, 256 devices: a whole 4x4x8 slice. The times are simulated.
256 devices in a mesh: section: 16 (over y, x), dp: 16 (over z, core).
Axes of the slice: x: 4, y: 4, z: 8, core: 2. Of those that a mesh axis runs over, the one named last changes fastest.
Arguments:
- hidden: bfloat16 [16, 256, 8192], P('dp', 'section'), may hold values from -1500 to 1500
- head: bfloat16 [65536, 8192], P('section', 'dp'), may hold values from -0.0625 to 0.0625
- block_id: int32 [16, 16], P(None, 'section'), may hold values from 0 to 7
- block_live: int32 [16, 16], P(None, 'section'), may hold values from 0 to 1, as said below
- teacher: bfloat16 [16, 256, 8192], P('dp', None, 'section'), may hold values from -400 to 400
Outputs:
- grad_hidden: bfloat16 [16, 256, 8192], P('dp', 'section')
- grad_head: bfloat16 [65536, 8192], P('section', 'dp')
Inputs may be any that keep to these rules, and one draw needn't show every extreme that they name: `block_live`: every micro-batch has at least one live section.
All inputs are finite; a program needn't handle non-finite values.
Results may differ from a plain program's by a relative error of at most 0.0056.
Values may be sent and summed in bfloat16 or wider, within the bound.
No kernel may reach another device: no remote copies, remote signals or barrier semaphores. Data moves between devices by JAX's collectives and lax.ppermute only.
A program may use at most 128 MiB of HBM per device.

v0:
```python
import jax
import jax.numpy as jnp
from jax import lax
from jax.sharding import PartitionSpec as P

neg_fill = -1e30


def local(hidden, head, block_id, block_live, teacher):
    my_replica = lax.axis_index("dp")
    tok_local = hidden.shape[1]
    model_width = hidden.shape[2]
    block_rows = teacher.shape[2]
    col_width = head.shape[1]
    blocks = head.shape[0] // block_rows
    table = head.reshape(blocks, block_rows, col_width)
    block_ids = block_id[:, 0]
    live_flags = block_live[:, 0]
    picked = jnp.take(table, block_ids, axis=0)
    whole = lax.all_gather(hidden, "section", axis=1, tiled=True)
    hidden_rows = whole[0]
    own_live = lax.dynamic_index_in_dim(live_flags, my_replica, 0, keepdims=False) > 0
    full_rows = lax.all_to_all(picked, "dp", split_axis=0, concat_axis=2, tiled=True)[0]
    logits = jnp.einsum("td,rd->tr", hidden_rows, full_rows, preferred_element_type=jnp.float32)
    teach = teacher[0].astype(jnp.float32)
    live_value = jnp.where(own_live, 1.0, 0.0).astype(jnp.float32)
    stud_local = jnp.where(own_live, jnp.max(logits, axis=1), neg_fill)
    teach_local = jnp.where(own_live, jnp.max(teach, axis=1), neg_fill)
    stud_top, teach_top = lax.pmax((stud_local, teach_local), "section")
    stud_part = jnp.where(own_live, jnp.sum(jnp.exp(logits - stud_top[:, None]), axis=1), 0.0)
    teach_part = jnp.where(own_live, jnp.sum(jnp.exp(teach - teach_top[:, None]), axis=1), 0.0)
    stud_total, teach_total, live_count = lax.psum((stud_part, teach_part, live_value), "section")
    student = jnp.where(own_live, jnp.exp(logits - stud_top[:, None]) / stud_total[:, None], 0.0)
    teach_prob = jnp.where(
        own_live, jnp.exp(teach - teach_top[:, None]) / teach_total[:, None], 0.0
    )
    logit_grad = (block_rows * live_count * (student - teach_prob)).astype(jnp.bfloat16)
    summed = lax.psum_scatter(
        jnp.dot(logit_grad, full_rows, preferred_element_type=jnp.float32),
        "section",
        scatter_dimension=0,
        tiled=True,
    )
    grad_hidden = summed.astype(jnp.bfloat16).reshape(1, tok_local, model_width)
    contrib = jnp.einsum(
        "tr,td->rd", logit_grad, hidden_rows, preferred_element_type=jnp.float32
    ).astype(jnp.bfloat16)
    returned = lax.all_to_all(contrib[None], "dp", split_axis=2, concat_axis=0, tiled=True)
    block_range = jnp.arange(blocks, dtype=jnp.int32)[None, :]
    selector = jnp.where(
        (live_flags[:, None] > 0) & (block_ids[:, None] == block_range), 1.0, 0.0
    ).astype(jnp.bfloat16)
    grad_head = jnp.einsum("mb,mrc->brc", selector, returned, preferred_element_type=jnp.float32)
    grad_head = grad_head.astype(jnp.bfloat16).reshape(blocks * block_rows, col_width)
    return (grad_hidden, grad_head)


def solution(mesh):
    placed = (
        P("dp", "section", None),
        P("section", "dp"),
        P(None, "section"),
        P(None, "section"),
        P("dp", None, "section"),
    )
    return jax.shard_map(
        local,
        mesh=mesh,
        in_specs=placed,
        out_specs=(P("dp", "section", None), P("section", "dp")),
        check_vma=False,
    )
```

profile of v0, /device:TPU:1, one launch (start us, length us, event | category | flops | bytes accessed | tf_op | source)
XLA Modules:
  0.0 687.1 jit_solution(2337014340000765486)
XLA Ops:
  7.2 0.7 fusion.26
  7.8 0.7 and_bitcast_fusion
  8.5 7.0 %gather_fusion = bf16[16,512,512]{2,1,0:T(8,128)(2,1)} fusion(bf16[8,512,512]{2,1,0:T(8,128)(2,1)} %bitcast.57, s32[1024]{0:T(1024)S(1)} %pad_clamp_fusion), kind=kCustom, calls=%fused_computation | custom fusion | bytes 16777280 | tf_op jit(solution)/shard_map/jit(_take)/gather | solution.py:19
  15.4 7.5 %broadcast_select_fusion = bf16[16,512,512]{2,1,0:T(8,128)(2,1)} fusion(bf16[16,512,512]{2,1,0:T(8,128)(2,1)} %gather_fusion, pred[16]{0:T(512)(128)(4,1)S(1)} %and_bitcast_fusion), kind=kLoop, calls=%fused_computation.5 | loop fusion | flops 4194304 | bytes 16777232 | tf_op jit(solution)/shard_map/jit(_take)/select_n | solution.py:19
  22.9 0.0 copy-start
  22.9 0.0 copy-start.2
  22.9 10.1 %all-to-all-start = ((bf16[16,512,512]{2,1,0:T(8,128)(2,1)}), bf16[16,512,512]{2,1,0:T(8,128)(2,1)}, u32[]{:S(2)}, u32[]{:S(2)}) async-start(bf16[16,512,512]{2,1,0:T(8,128)(2,1)} %broadcast_select_fusion), calls=%async_computation | async-start | bytes 16777216 | tf_op jit(solution)/shard_map/all_to_all | solution.py:23
  33.0 0.0 all-gather.2.cloned.1.call-start
  33.1 0.7 all-gather.2.cloned.1.call-update
  33.8 0.0 reduce-scatter.2.cloned.1.call-start
  33.8 0.0 copy-done
  33.8 0.1 copy.14
  34.0 0.1 reduce_max.24
  34.1 0.0 copy-done.2
  34.1 0.6 fusion.30
  35.3 181.2 %all-to-all-done = bf16[16,512,512]{2,1,0:T(8,128)(2,1)} async-done(((bf16[16,512,512]{2,1,0:T(8,128)(2,1)}), bf16[16,512,512]{2,1,0:T(8,128)(2,1)}, u32[]{:S(2)}, u32[]{:S(2)}) %all-to-all-start) | async-done | bytes 8388640 | tf_op jit(solution)/shard_map/all_to_all | solution.py:23
  216.6 12.3 %copy.13 = bf16[1,512,16,512]{1,3,2,0:T(8,128)(2,1)} copy(bf16[1,512,16,512]{3,1,2,0:T(8,128)(2,1)} %bitcast.5) | data formatting | bytes 16777216 | tf_op jit(solution)/shard_map/all_to_all | solution.py:23
  228.9 0.0 all-gather.2.cloned.1.call-done
  228.9 7.0 %fusion.31 = (f32[256]{0:T(256)S(1)}, f32[512,256]{1,0:T(8,128)S(1)}) fusion(bf16[512,8192]{0,1:T(8,128)(2,1)} %bitcast.55, bf16[1,256,8192]{2,1,0:T(8,128)(2,1)} %all-gather.2.cloned.1.call-done), kind=kOutput, calls=%fused_computation.43 | convolution fusion | flops 2147614464 | bytes 13108224 | tf_op jit(solution)/shard_map/td,rd->tr/dot_general | solution.py:24
  235.8 0.7 convert_select_fusion
  236.5 33.4 %all-reduce.1 = (f32[256]{0:T(256)S(1)}, f32[256]{0:T(256)S(1)}) all-reduce(f32[256]{0:T(256)S(1)} %get-tuple-element.9, f32[256]{0:T(256)S(1)} %get-tuple-element.10), channel_id=1, replica_groups=mesh['section'=16,'dp'=16] {'section'}, use_global_device_ids=true, to_apply=%region_6.7 | all-reduce | flops 512 | bytes 4096 | tf_op jit(solution)/shard_map/pmax | solution.py:29
  269.9 0.1 fusion.11
  270.0 0.6 broadcast_select_fusion.1
  270.7 0.1 fusion.16
  270.8 0.6 broadcast_select_fusion.2
  271.5 29.2 %all-reduce = (f32[256]{0:T(256)S(1)}, f32[256]{0:T(256)S(1)}, f32[]{:T(128)}) all-reduce(f32[256]{0:T(256)S(1)} %broadcast_select_fusion.1, f32[256]{0:T(256)S(1)} %broadcast_select_fusion.2, f32[]{:T(128)S(6)} %select_n.61), channel_id=1, replica_groups=mesh['section'=16,'dp'=16] {'section'}, use_global_device_ids=true, to_apply=%region_8.9 | all-reduce | flops 513 | bytes 4104 | tf_op jit(solution)/shard_map/psum | solution.py:32
  301.3 9.8 %fusion.28 = f32[256,8192]{1,0:T(8,128)} fusion(bf16[512,8192]{0,1:T(8,128)(2,1)} %bitcast.56, f32[512,256]{1,0:T(8,128)S(1)} %get-tuple-element.8, bf16[1,256,512]{1,2,0:T(8,128)(2,1)S(1)} %copy.14, f32[256]{0:T(256)S(1)} %get-tuple-element.2, f32[256]{0:T(256)S(1)} %get-tuple-element.5, f32[256]{0:T(256)S(1)} %get-tuple-element.3, ...), kind=kOutput, calls=%fused_computation.41 | convolution fusion | flops 2148794368 | bytes 17567748 | tf_op jit(solution)/shard_map/dot_general | solution.py:39
  311.2 0.0 reduce-scatter.2.cloned.1.call-update
  311.2 8.5 %fusion = bf16[1,512,8192]{2,1,0:T(8,128)(2,1)} fusion(bf16[1,256,8192]{2,1,0:T(8,128)(2,1)} %all-gather.2.cloned.1.call-done, f32[512,256]{1,0:T(8,128)S(1)} %get-tuple-element.8, bf16[1,256,512]{1,2,0:T(8,128)(2,1)S(1)} %copy.14, f32[256]{0:T(256)S(1)} %get-tuple-element.2, f32[256]{0:T(256)S(1)} %get-tuple-element.5, f32[256]{0:T(256)S(1)} %get-tuple-element.3, ...), kind=kOutput, calls=%fused_computation.2 | convolution fusion | flops 2152988672 | bytes 13373445 | tf_op jit(solution)/shard_map/tr,td->rd/dot_general | solution.py:45
  319.7 34.7 %copy.15 = bf16[1,512,8192]{1,0,2:T(2,128)(2,1)} copy(bf16[1,512,8192]{2,1,0:T(8,128)(2,1)} %fusion) | data formatting | bytes 16777216 | tf_op jit(solution)/shard_map/broadcast_in_dim | solution.py:48
  354.5 0.5 broadcast.31
  355.0 54.7 %reduce.4 = bf16[8192,512]{1,0:T(8,128)(2,1)} reduce(bf16[8192,1,512]{2,1,0:T(2,128)(2,1)} %bitcast.53, bf16[]{:T(256)} %broadcast.31), dimensions={1}, to_apply=%bitcast.46.reduce_sub_computation | reduce | bytes 16777218
  409.6 14.6 %reshape.42 = bf16[16,2,131072]{2,1,0:T(2,128)(2,1)} reshape(bf16[8192,512]{1,0:T(8,128)(2,1)} %reduce.4) | data formatting | bytes 16777216
  424.3 19.7 %all-to-all-start.1 = ((bf16[16,2,131072]{2,1,0:T(2,128)(2,1)}), bf16[16,2,131072]{2,1,0:T(2,128)(2,1)}, u32[]{:S(2)}, u32[]{:S(2)}) async-start(bf16[16,2,131072]{2,1,0:T(2,128)(2,1)} %reshape.42), calls=%async_computation.2 | async-start | bytes 16777216 | tf_op jit(solution)/shard_map/all_to_all | solution.py:48
  443.9 183.5 %all-to-all-done.1 = bf16[16,2,131072]{2,1,0:T(2,128)(2,1)} async-done(((bf16[16,2,131072]{2,1,0:T(2,128)(2,1)}), bf16[16,2,131072]{2,1,0:T(2,128)(2,1)}, u32[]{:S(2)}, u32[]{:S(2)}) %all-to-all-start.1) | async-done | bytes 8388640 | tf_op jit(solution)/shard_map/all_to_all | solution.py:48
  627.4 16.5 %reshape.43 = bf16[8192,1,512]{2,1,0:T(2,128)(2,1)} reshape(bf16[16,2,131072]{2,1,0:T(2,128)(2,1)} %all-to-all-done.1) | data formatting | bytes 16777216
  643.9 11.6 %copy.19 = bf16[1,512,8192]{1,2,0:T(8,128)(2,1)} copy(bf16[1,512,8192]{1,0,2:T(2,128)(2,1)} %bitcast.52) | data formatting | bytes 16777216
  655.5 0.0 copy-start.1
  655.5 14.9 %copy.18 = bf16[1,512,16,512]{3,2,1,0:T(8,128)(2,1)} copy(bf16[1,512,16,512]{1,3,2,0:T(8,128)(2,1)} %bitcast.54) | data formatting | bytes 16777216 | tf_op jit(solution)/shard_map/all_to_all | solution.py:48
  670.4 0.0 copy-done.1
  670.4 4.6 fusion.6
  675.1 3.5 copy.17
  678.5 0.0 reduce-scatter.2.cloned.1.call-done
  678.5 1.8 convert_bitcast_fusion
  (2 shorter events, 0.0 us)
Async XLA Ops:
  22.9 10.9 %copy-start = (bf16[1,256,512]{2,1,0:T(8,128)(2,1)S(1)}, bf16[1,256,512]{2,1,0:T(8,128)(2,1)}, u32[]{:S(2)}) copy-start(bf16[1,256,512]{2,1,0:T(8,128)(2,1)} %param.9) | copy-start | bytes 786436
  22.9 11.2 %copy-start.2 = (s32[16,1]{0,1:T(1,128)S(1)}, s32[16,1]{0,1:T(1,128)}, u32[]{:S(2)}) copy-start(s32[16,1]{0,1:T(1,128)} %param.8) | copy-start | bytes 196
  22.9 193.6 %all-to-all-start = ((bf16[16,512,512]{2,1,0:T(8,128)(2,1)}), bf16[16,512,512]{2,1,0:T(8,128)(2,1)}, u32[]{:S(2)}, u32[]{:S(2)}) async-start(bf16[16,512,512]{2,1,0:T(8,128)(2,1)} %broadcast_select_fusion), calls=%async_computation | async-start | bytes 16777216 | tf_op jit(solution)/shard_map/all_to_all | solution.py:23
  33.0 195.8 %all-gather.2.cloned.1.call-start = ((), (), s32[]{:S(2)}) async-start(), calls=%async_computation.3 | async-start | bytes 4456448 | tf_op jit(solution)/shard_map/all_gather | solution.py:20
  33.8 644.8 %reduce-scatter.2.cloned.1.call-start = ((), (), s32[]{:S(2)}) async-start(), calls=%async_computation.4 | async-start | bytes 8912896 | tf_op jit(solution)/shard_map/reduce_scatter | solution.py:38
  424.3 203.1 %all-to-all-start.1 = ((bf16[16,2,131072]{2,1,0:T(2,128)(2,1)}), bf16[16,2,131072]{2,1,0:T(2,128)(2,1)}, u32[]{:S(2)}, u32[]{:S(2)}) async-start(bf16[16,2,131072]{2,1,0:T(2,128)(2,1)} %reshape.42), calls=%async_computation.2 | async-start | bytes 16777216 | tf_op jit(solution)/shard_map/all_to_all | solution.py:48
  655.5 14.9 %copy-start.1 = (s32[16,1]{0,1:T(1,128)S(1)}, s32[16,1]{0,1:T(1,128)}, u32[]{:S(2)}) copy-start(s32[16,1]{0,1:T(1,128)} %param.7) | copy-start | bytes 196
Sparse Core Ops, SparseCore 0:
  36.3 57.5 all-gather.1
  311.3 98.5 reduce-scatter.1
where the time goes:
time: 690 us; the launch traced here: 687 us
  waiting for transfers between devices  365 us (53%)
  local copies, waits for them, and re-layouts  116 us (17%)
  other arithmetic  68.1 us (10%)
  blocking collectives  62.6 us (9%)
  matrix products  30 us (4%)
  starting transfers between devices  29.8 us (4%)
  between operations  15.4 us (2%)
    all_to_all x1, waiting for transfers between devices, local(): lax.all_to_all(contrib[None], 'dp', split_axis=2, concat_axis=0, tiled=True)  183 us
    all_to_all x1, waiting for transfers between devices, local(): lax.all_to_all(picked, 'dp', split_axis=0, concat_axis=2, tiled=True)[0]  181 us
    unnamed x1, other arithmetic  54.7 us
    unnamed x11, local copies, waits for them, and re-layouts  43.4 us
    broadcast_in_dim x1, local copies, waits for them, and re-layouts, local(): contrib[None]  34.7 us
    pmax x1, blocking collectives, local(): stud_top, teach_top = lax.pmax((stud_local, teach_local), 'section')  33.4 us
    psum x1, blocking collectives, local(): lax.psum((stud_part, teach_part, live_value), 'section')  29.2 us
    all_to_all x1, starting transfers between devices, local(): lax.all_to_all(contrib[None], 'dp', split_axis=2, concat_axis=0, tiled=True)  19.7 us
  transfers between devices with their start and end apart: 4, of which 2 were waited for; matrix products, arithmetic and copies ran while one was open for 26% of the time, Pallas kernels for 0%

commit v1 on v0

--- a/solution.py
+++ b/solution.py
@@ -20,7 +20,10 @@
     whole = lax.all_gather(hidden, "section", axis=1, tiled=True)
     hidden_rows = whole[0]
     own_live = lax.dynamic_index_in_dim(live_flags, my_replica, 0, keepdims=False) > 0
-    full_rows = lax.all_to_all(picked, "dp", split_axis=0, concat_axis=2, tiled=True)[0]
+    full_rows = jnp.concatenate(
+        lax.all_to_all(jnp.stack(jnp.split(picked, lax.axis_size("dp"), axis=0)), "dp", 0, 0),
+        axis=2,
+    )[0]
     logits = jnp.einsum("td,rd->tr", hidden_rows, full_rows, preferred_element_type=jnp.float32)
     teach = teacher[0].astype(jnp.float32)
     live_value = jnp.where(own_live, 1.0, 0.0).astype(jnp.float32)

time: 690 us -> 721 us (1.045)
  local copies, waits for them, and re-layouts: 116 us -> 146 us
    unnamed x11 -> x26, local copies, waits for them, and re-layouts: 43.4 us -> 71.6 us
    all_to_all x1 -> x0, local copies, waits for them, and re-layouts: 12.3 us -> none  [local(): lax.all_to_all(picked, 'dp', split_axis=0, concat_axis=2, tiled=True)[0]]
    reshape x0 -> x1, local copies, waits for them, and re-layouts: none -> 12.3 us  [local(): jnp.concatenate(lax.all_to_all(jnp.stack(jnp.split(picked, lax.axis_size(...]
  transfers between devices with their start and end apart: 4 -> 4, of which waited for: 2 -> 2; matrix products, arithmetic and copies ran while one was open for 26% -> 25% of each run, Pallas kernels for 0% -> 0%
where the time goes in v1:
time: 721 us; the launch traced here: 717 us
  waiting for transfers between devices  365 us (51%)
  local copies, waits for them, and re-layouts  146 us (20%)
  other arithmetic  68.1 us (9%)
  blocking collectives  62.6 us (9%)
  matrix products  29.9 us (4%)
  starting transfers between devices  29.8 us (4%)
  between operations  15.4 us (2%)
    all_to_all x1, waiting for transfers between devices, local(): lax.all_to_all(contrib[None], 'dp', split_axis=2, concat_axis=0, tiled=True)  183 us
    all_to_all x1, waiting for transfers between devices, local(): lax.all_to_all(jnp.stack(jnp.split(picked, lax.axis_size('dp'), axis=0)),...  181 us
    unnamed x26, local copies, waits for them, and re-layouts  71.6 us
    unnamed x1, other arithmetic  54.7 us
    broadcast_in_dim x1, local copies, waits for them, and re-layouts, local(): contrib[None]  34.7 us
    pmax x1, blocking collectives, local(): stud_top, teach_top = lax.pmax((stud_local, teach_local), 'section')  33.4 us
    psum x1, blocking collectives, local(): lax.psum((stud_part, teach_part, live_value), 'section')  29.2 us
    all_to_all x1, starting transfers between devices, local(): lax.all_to_all(contrib[None], 'dp', split_axis=2, concat_axis=0, tiled=True)  19.7 us
  transfers between devices with their start and end apart: 4, of which 2 were waited for; matrix products, arithmetic and copies ran while one was open for 25% of the time, Pallas kernels for 0%

profile of v1, /device:TPU:1, one launch (start us, length us, event | category | flops | bytes accessed | tf_op | source)
XLA Modules:
  0.0 717.2 jit_solution(5863932435049776504)
XLA Ops:
  7.2 0.7 fusion.42
  7.8 0.7 and_bitcast_fusion
  8.5 6.9 gather_fusion
  15.4 7.5 %broadcast_select_fusion = bf16[16,512,512]{2,1,0:T(8,128)(2,1)} fusion(bf16[16,512,512]{2,1,0:T(8,128)(2,1)} %gather_fusion, pred[16]{0:T(512)(128)(4,1)S(1)} %and_bitcast_fusion), kind=kLoop, calls=%fused_computation.5 | loop fusion | flops 4194304 | bytes 16777232 | tf_op jit(solution)/shard_map/jit(_take)/select_n | solution.py:19
  22.9 1.9 fusion.24
  24.8 1.9 fusion.23
  26.6 1.9 fusion.22
  28.5 1.9 fusion.21
  30.4 1.9 fusion.20
  32.3 1.9 fusion.19
  34.2 1.9 fusion.18
  36.0 1.9 fusion.17
  37.9 1.9 fusion.16
  39.8 1.9 fusion.15
  41.7 1.9 fusion.14
  43.6 1.9 fusion.13
  45.5 1.9 fusion.12
  47.3 1.9 fusion.11
  49.2 1.9 fusion.10
  51.1 1.9 fusion.9
  53.0 10.1 %all-to-all-start = ((bf16[16,1,512,512]{3,2,1,0:T(8,128)(2,1)}), bf16[16,1,512,512]{3,2,1,0:T(8,128)(2,1)}, u32[]{:S(2)}, u32[]{:S(2)}) async-start(bf16[16,1,512,512]{3,2,1,0:T(8,128)(2,1)} %fusion.9), calls=%async_computation | async-start | bytes 16777216 | tf_op jit(solution)/shard_map/all_to_all | solution.py:24
  63.1 0.7 all-gather.2.cloned.1.call-update
  63.9 0.1 copy.29
  64.2 0.6 fusion.46
  65.4 181.2 %all-to-all-done = bf16[16,1,512,512]{3,2,1,0:T(8,128)(2,1)} async-done(((bf16[16,1,512,512]{3,2,1,0:T(8,128)(2,1)}), bf16[16,1,512,512]{3,2,1,0:T(8,128)(2,1)}, u32[]{:S(2)}, u32[]{:S(2)}) %all-to-all-start) | async-done | bytes 8388640 | tf_op jit(solution)/shard_map/all_to_all | solution.py:24
  246.6 12.3 %copy.28 = bf16[1,512,16,512]{1,3,2,0:T(8,128)(2,1)} copy(bf16[1,512,16,512]{3,1,0,2:T(8,128)(2,1)} %bitcast.20) | data formatting | bytes 16777216 | tf_op jit(solution)/shard_map/reshape | solution.py:23
  258.9 7.0 fusion.47
  265.9 0.7 convert_select_fusion
  266.6 33.4 %all-reduce.1 = (f32[256]{0:T(256)S(1)}, f32[256]{0:T(256)S(1)}) all-reduce(f32[256]{0:T(256)S(1)} %get-tuple-element.9, f32[256]{0:T(256)S(1)} %get-tuple-element.10), channel_id=1, replica_groups=mesh['section'=16,'dp'=16] {'section'}, use_global_device_ids=true, to_apply=%region_6.7 | all-reduce | flops 512 | bytes 4096 | tf_op jit(solution)/shard_map/pmax | solution.py:32
  300.0 0.1 fusion.27
  300.1 0.6 broadcast_select_fusion.1
  300.8 0.1 fusion.32
  300.9 0.6 broadcast_select_fusion.2
  301.6 29.2 %all-reduce = (f32[256]{0:T(256)S(1)}, f32[256]{0:T(256)S(1)}, f32[]{:T(128)}) all-reduce(f32[256]{0:T(256)S(1)} %broadcast_select_fusion.1, f32[256]{0:T(256)S(1)} %broadcast_select_fusion.2, f32[]{:T(128)S(6)} %select_n.61), channel_id=1, replica_groups=mesh['section'=16,'dp'=16] {'section'}, use_global_device_ids=true, to_apply=%region_8.9 | all-reduce | flops 513 | bytes 4104 | tf_op jit(solution)/shard_map/psum | solution.py:35
  331.4 9.8 %fusion.44 = f32[256,8192]{1,0:T(8,128)} fusion(bf16[512,8192]{0,1:T(8,128)(2,1)} %bitcast.118, f32[512,256]{1,0:T(8,128)S(1)} %get-tuple-element.8, bf16[1,256,512]{1,2,0:T(8,128)(2,1)S(1)} %copy.29, f32[256]{0:T(256)S(1)} %get-tuple-element.2, f32[256]{0:T(256)S(1)} %get-tuple-element.5, f32[256]{0:T(256)S(1)} %get-tuple-element.3, ...), kind=kOutput, calls=%fused_computation.73 | convolution fusion | flops 2148794368 | bytes 17567748 | tf_op jit(solution)/shard_map/dot_general | solution.py:42
  341.3 8.5 %fusion = bf16[1,512,8192]{2,1,0:T(8,128)(2,1)} fusion(bf16[1,256,8192]{2,1,0:T(8,128)(2,1)} %all-gather.2.cloned.1.call-done, f32[512,256]{1,0:T(8,128)S(1)} %get-tuple-element.8, bf16[1,256,512]{1,2,0:T(8,128)(2,1)S(1)} %copy.29, f32[256]{0:T(256)S(1)} %get-tuple-element.2, f32[256]{0:T(256)S(1)} %get-tuple-element.5, f32[256]{0:T(256)S(1)} %get-tuple-element.3, ...), kind=kOutput, calls=%fused_computation.2 | convolution fusion | flops 2152988672 | bytes 13373445 | tf_op jit(solution)/shard_map/tr,td->rd/dot_general | solution.py:48
  349.8 34.7 %copy.30 = bf16[1,512,8192]{1,0,2:T(2,128)(2,1)} copy(bf16[1,512,8192]{2,1,0:T(8,128)(2,1)} %fusion) | data formatting | bytes 16777216 | tf_op jit(solution)/shard_map/broadcast_in_dim | solution.py:51
  384.5 0.5 broadcast.31
  385.1 54.7 %reduce.4 = bf16[8192,512]{1,0:T(8,128)(2,1)} reduce(bf16[8192,1,512]{2,1,0:T(2,128)(2,1)} %bitcast.115, bf16[]{:T(256)} %broadcast.31), dimensions={1}, to_apply=%bitcast.108.reduce_sub_computation | reduce | bytes 16777218
  439.7 14.6 %reshape.45 = bf16[16,2,131072]{2,1,0:T(2,128)(2,1)} reshape(bf16[8192,512]{1,0:T(8,128)(2,1)} %reduce.4) | data formatting | bytes 16777216
  454.3 19.7 %all-to-all-start.1 = ((bf16[16,2,131072]{2,1,0:T(2,128)(2,1)}), bf16[16,2,131072]{2,1,0:T(2,128)(2,1)}, u32[]{:S(2)}, u32[]{:S(2)}) async-start(bf16[16,2,131072]{2,1,0:T(2,128)(2,1)} %reshape.45), calls=%async_computation.2 | async-start | bytes 16777216 | tf_op jit(solution)/shard_map/all_to_all | solution.py:51
  474.0 183.5 %all-to-all-done.1 = bf16[16,2,131072]{2,1,0:T(2,128)(2,1)} async-done(((bf16[16,2,131072]{2,1,0:T(2,128)(2,1)}), bf16[16,2,131072]{2,1,0:T(2,128)(2,1)}, u32[]{:S(2)}, u32[]{:S(2)}) %all-to-all-start.1) | async-done | bytes 8388640 | tf_op jit(solution)/shard_map/all_to_all | solution.py:51
  657.5 16.5 %reshape.46 = bf16[8192,1,512]{2,1,0:T(2,128)(2,1)} reshape(bf16[16,2,131072]{2,1,0:T(2,128)(2,1)} %all-to-all-done.1) | data formatting | bytes 16777216
  674.0 11.6 %copy.34 = bf16[1,512,8192]{1,2,0:T(8,128)(2,1)} copy(bf16[1,512,8192]{1,0,2:T(2,128)(2,1)} %bitcast.114) | data formatting | bytes 16777216
  685.6 14.9 %copy.33 = bf16[1,512,16,512]{3,2,1,0:T(8,128)(2,1)} copy(bf16[1,512,16,512]{1,3,2,0:T(8,128)(2,1)} %bitcast.116) | data formatting | bytes 16777216 | tf_op jit(solution)/shard_map/all_to_all | solution.py:51
  700.5 4.6 fusion.6
  705.1 3.5 copy.32
  708.6 1.8 convert_bitcast_fusion
  (14 shorter events, 0.2 us)
Async XLA Ops:
  53.0 10.9 %copy-start = (bf16[1,256,512]{2,1,0:T(8,128)(2,1)S(1)}, bf16[1,256,512]{2,1,0:T(8,128)(2,1)}, u32[]{:S(2)}) copy-start(bf16[1,256,512]{2,1,0:T(8,128)(2,1)} %param.9) | copy-start | bytes 786436
  53.0 11.2 %copy-start.2 = (s32[16,1]{0,1:T(1,128)S(1)}, s32[16,1]{0,1:T(1,128)}, u32[]{:S(2)}) copy-start(s32[16,1]{0,1:T(1,128)} %param.8) | copy-start | bytes 196
  53.0 193.6 %all-to-all-start = ((bf16[16,1,512,512]{3,2,1,0:T(8,128)(2,1)}), bf16[16,1,512,512]{3,2,1,0:T(8,128)(2,1)}, u32[]{:S(2)}, u32[]{:S(2)}) async-start(bf16[16,1,512,512]{3,2,1,0:T(8,128)(2,1)} %fusion.9), calls=%async_computation | async-start | bytes 16777216 | tf_op jit(solution)/shard_map/all_to_all | solution.py:24
  63.1 195.8 %all-gather.2.cloned.1.call-start = ((), (), s32[]{:S(2)}) async-start(), calls=%async_computation.3 | async-start | bytes 4456448 | tf_op jit(solution)/shard_map/all_gather | solution.py:20
  63.8 644.8 %reduce-scatter.2.cloned.1.call-start = ((), (), s32[]{:S(2)}) async-start(), calls=%async_computation.4 | async-start | bytes 8912896 | tf_op jit(solution)/shard_map/reduce_scatter | solution.py:41
  454.3 203.1 %all-to-all-start.1 = ((bf16[16,2,131072]{2,1,0:T(2,128)(2,1)}), bf16[16,2,131072]{2,1,0:T(2,128)(2,1)}, u32[]{:S(2)}, u32[]{:S(2)}) async-start(bf16[16,2,131072]{2,1,0:T(2,128)(2,1)} %reshape.45), calls=%async_computation.2 | async-start | bytes 16777216 | tf_op jit(solution)/shard_map/all_to_all | solution.py:51
  685.6 14.9 %copy-start.1 = (s32[16,1]{0,1:T(1,128)S(1)}, s32[16,1]{0,1:T(1,128)}, u32[]{:S(2)}) copy-start(s32[16,1]{0,1:T(1,128)} %param.7) | copy-start | bytes 196
Sparse Core Ops, SparseCore 0:
  66.4 57.5 all-gather.1
  341.4 98.5 reduce-scatter.1
